TPU v7x, 32 devices: a whole 2x2x4 slice. The times are simulated.
32 devices in a mesh: ctx: 4 (over y, x), pair: 4 (over z), dp: 2 (over core).
Axes of the slice: x: 2, y: 2, z: 4, core: 2. Of those that a mesh axis runs over, the one named last changes fastest.
Arguments:
- queries: bfloat16 [8, 4, 128, 2048], P(('dp', 'ctx'), 'pair'), parts along dimension 0, may hold values from -8 to 8
- resp_keys: bfloat16 [8, 4, 128, 1024], P(('dp', 'ctx'), 'pair'), parts along dimension 0, may hold values from -6 to 6
- resp_values: bfloat16 [8, 4, 128, 1024], P(('dp', 'ctx'), 'pair'), parts along dimension 0, may hold values from -6 to 6
- d_out: bfloat16 [8, 4, 128, 2048], P(('dp', 'ctx'), 'pair'), parts along dimension 0, may hold values from -6 to 6
- prefix_kv: bfloat16 [4, 512, 2, 1024], P('dp', 'ctx', None, 'pair'), parts along dimension 0, may hold values from -8 to 8
- prefix_blocks: int32 [8, 4, 4], P(('dp', 'ctx'), 'pair'), parts along dimension 0, may hold values 0 or 1
- resp_lengths: int32 [8, 4], P(('dp', 'ctx'), 'pair'), parts along dimension 0, may hold values from 32 to 128, as said below
- pair_prompt: int32 [8], P('dp'), parts along dimension 0, may hold values from 0 to 1, as said below
Outputs:
- d_queries: bfloat16 [8, 4, 128, 2048], P(('dp', 'ctx'), 'pair'), parts along dimension 0
- d_resp_keys: bfloat16 [8, 4, 128, 1024], P(('dp', 'ctx'), 'pair'), parts along dimension 0
- d_resp_values: bfloat16 [8, 4, 128, 1024], P(('dp', 'ctx'), 'pair'), parts along dimension 0
- d_prefix: float32 [4, 512, 2, 1024], P('dp', 'ctx', None, 'pair'), parts along dimension 0
There are 2 independent parts, one for each index of `dp`. A program takes and returns all parts, laid end to end along the dimension named above; each array names one. Nothing has to cross between parts.
Inputs may be any that keep to these rules, and one draw needn't show every extreme that they name: `pair_prompt`: each prompt is answered by exactly two indices of pair, one chosen and one rejected response. `resp_lengths`: some response fills all 128 slots.
All inputs are finite; a program needn't handle non-finite values. No bound on the sum of `prefix_blocks` on one device may be relied on, other than what follows from the above.
Results may differ from a plain program's by a relative error of at most 0.012.
The roundings to bfloat16 on the way count: a program that leaves them out, or rounds other values in their place, can miss the bound.
Values may be sent and summed in bfloat16 or wider, within the bound.
No kernel may reach another device: no remote copies, remote signals or barrier semaphores. Data moves between devices by JAX's collectives and lax.ppermute only.
A program may use at most 128 MiB of HBM per device.

v0:
```python
import jax
import jax.numpy as jnp
from jax import lax
from jax.sharding import PartitionSpec as P

KV_HEADS = 8
GROUP = 2
HEAD_DIM = 128
BLOCK = 128
scale_factor = 144.0 ** (-0.5)
neg_big = -1e30


def gather_rows(kv_part):
    return lax.all_gather(kv_part, "ctx", axis=1, tiled=True)


def pick_prompt(kv_part, pair_prompt):
    outgoing = jnp.take(kv_part, pair_prompt, axis=0)
    return lax.all_to_all(outgoing, "pair", split_axis=0, concat_axis=3, tiled=True)


def shards(
    queries, resp_keys, resp_values, d_out, prefix_kv, prefix_blocks, resp_lengths, pair_prompt
):
    prefix_panel = gather_rows(pick_prompt(prefix_kv, pair_prompt))
    prefix_panel = prefix_panel[0]
    resp_rows = queries.shape[2]
    pre_rows = prefix_panel.shape[0]
    n_prompts = prefix_kv.shape[0]
    all_rows = pre_rows + resp_rows
    keys_heads = jnp.transpose(
        jnp.concatenate([prefix_panel[:, 0], resp_keys[0, 0]], 0).reshape(
            all_rows, KV_HEADS, HEAD_DIM
        ),
        (1, 0, 2),
    )
    values_heads = jnp.transpose(
        jnp.concatenate([prefix_panel[:, 1], resp_values[0, 0]], 0).reshape(
            all_rows, KV_HEADS, HEAD_DIM
        ),
        (1, 0, 2),
    )
    query_heads = jnp.transpose(
        queries[0, 0].reshape(resp_rows, KV_HEADS, GROUP, HEAD_DIM), (1, 2, 0, 3)
    )
    positions = jnp.arange(resp_rows, dtype=jnp.int32)
    live_rows = positions < resp_lengths[0, 0]
    grad_rows = jnp.where(live_rows[:, None], d_out[0, 0], jnp.zeros_like(d_out[0, 0]))
    grad_heads = jnp.transpose(
        grad_rows.reshape(resp_rows, KV_HEADS, GROUP, HEAD_DIM), (1, 2, 0, 3)
    )
    visible = prefix_blocks[0, 0] > 0
    prefix_mask = jnp.broadcast_to(visible[:, None], (pre_rows // BLOCK, BLOCK)).reshape(pre_rows)
    causal = positions[:, None] >= positions[None, :]
    allowed = jnp.concatenate(
        [jnp.broadcast_to(prefix_mask[None, :], (resp_rows, pre_rows)), causal], 1
    )

    def one_head(items):
        key_rows, value_rows, query_rows, grad_part = items
        scores = (
            jnp.einsum("jqd,kd->jqk", query_rows, key_rows, preferred_element_type=jnp.float32)
            * scale_factor
        )
        scores = jnp.where(allowed[None], scores, neg_big)
        row_peak = jnp.max(scores, axis=-1, keepdims=True)
        raised = jnp.exp(scores - row_peak)
        weights = raised / jnp.sum(raised, axis=-1, keepdims=True)
        probs_low = weights.astype(jnp.bfloat16)
        attended = jnp.einsum(
            "jqk,kd->jqd", probs_low, value_rows, preferred_element_type=jnp.float32
        )
        attended = lax.optimization_barrier(attended.astype(jnp.bfloat16)).astype(jnp.float32)
        row_delta = jnp.sum(grad_part.astype(jnp.float32) * attended, axis=-1)
        d_probs = jnp.einsum(
            "jqd,kd->jqk", grad_part, value_rows, preferred_element_type=jnp.float32
        )
        ds_low = (weights * (d_probs - row_delta[..., None])).astype(jnp.bfloat16)
        query_grad = (
            jnp.einsum("jqk,kd->jqd", ds_low, key_rows, preferred_element_type=jnp.float32)
            * scale_factor
        )
        key_grad = (
            jnp.einsum("jqk,jqd->kd", ds_low, query_rows, preferred_element_type=jnp.float32)
            * scale_factor
        )
        value_grad = jnp.einsum(
            "jqk,jqd->kd", probs_low, grad_part, preferred_element_type=jnp.float32
        )
        both_grads = jnp.stack([key_grad, value_grad], 1).astype(jnp.bfloat16)
        return (query_grad.astype(jnp.bfloat16), both_grads)

    query_grads, kv_grads = lax.map(one_head, (keys_heads, values_heads, query_heads, grad_heads))
    d_queries = jnp.transpose(query_grads, (2, 0, 1, 3)).reshape(1, 1, resp_rows, -1)
    own_grads = jnp.transpose(kv_grads[:, pre_rows:], (1, 2, 0, 3)).reshape(resp_rows, 2, -1)
    d_resp_keys = own_grads[:, 0].reshape(1, 1, resp_rows, -1)
    d_resp_values = own_grads[:, 1].reshape(1, 1, resp_rows, -1)
    prefix_part = jnp.transpose(kv_grads[:, :pre_rows], (1, 2, 0, 3)).reshape(1, pre_rows, 2, -1)
    pieces = lax.all_to_all(prefix_part, "ctx", split_axis=1, concat_axis=0, tiled=True)
    ctx_total = jnp.sum(pieces.astype(jnp.float32), axis=0).astype(jnp.bfloat16)
    arrived = lax.all_to_all(ctx_total[None], "pair", split_axis=3, concat_axis=0, tiled=True)
    prompt_hits = (pair_prompt[:, None] == jnp.arange(n_prompts, dtype=jnp.int32)[None, :]).astype(
        jnp.float32
    )
    d_prefix = jnp.sum(
        prompt_hits[:, :, None, None, None] * arrived.astype(jnp.float32)[:, None], axis=0
    )
    return (d_queries, d_resp_keys, d_resp_values, d_prefix)


def solution(mesh):
    placed = (
        P(("dp", "ctx"), "pair", None, None),
        P(("dp", "ctx"), "pair", None, None),
        P(("dp", "ctx"), "pair", None, None),
        P(("dp", "ctx"), "pair", None, None),
        P("dp", "ctx", None, "pair"),
        P(("dp", "ctx"), "pair", None),
        P(("dp", "ctx"), "pair"),
        P("dp"),
    )
    return jax.shard_map(
        shards,
        mesh=mesh,
        in_specs=placed,
        out_specs=(
            P(("dp", "ctx"), "pair", None, None),
            P(("dp", "ctx"), "pair", None, None),
            P(("dp", "ctx"), "pair", None, None),
            P("dp", "ctx", None, "pair"),
        ),
        check_vma=False,
    )
```

profile of v0, /device:TPU:0, one launch (start us, length us, event | category | flops | bytes accessed | tf_op | source)
XLA Modules:
  0.0 192.6 jit_solution(804473975615161115)
XLA Ops:
  8.6 1.6 gather_fusion
  10.8 20.7 %all_to_all.39 = bf16[4,128,2,256]{3,2,1,0:T(2,128)(2,1)S(1)} all-to-all(bf16[4,128,2,256]{3,2,1,0:T(2,128)(2,1)S(1)} %broadcast_select_fusion), channel_id=1, replica_groups=mesh['ctx'=4,'pair'=4,'dp'=2] {'pair'}, dimensions={0} | all-to-all | bytes 1048576 | tf_op jit(solution)/shard_map/all_to_all | solution.py:20
  35.3 31.8 %all-gather.2.cloned.1.call-done = bf16[1,512,2,1024]{1,3,2,0:T(8,128)(2,1)} async-done(((bf16[1,128,2,1024]{1,3,2,0:T(8,128)(2,1)}), bf16[1,512,2,1024]{1,3,2,0:T(8,128)(2,1)}) %all-gather.2.cloned.1.call-update) | async-done | bytes 2097168 | tf_op jit(solution)/shard_map/all_gather | solution.py:15
  67.1 1.7 fusion.55
  68.7 1.3 maximum_bitcast_fusion
  70.1 50.9 %while.12 = (s32[]{:T(128)}, bf16[8,2,128,128]{3,2,1,0:T(8,128)(2,1)}, bf16[8,640,2,128]{3,1,2,0:T(8,128)(2,1)}, pred[128,640]{1,0:T(8,128)(4,1)S(1)}, bf16[8,2,...) while((s32[]{:T(128)}, ...), condition=%wide.region_4.5_spmd, body=%wide.region_0.4_spmd.sunk | while | flops 254427520 | bytes 6446201 | solution.py:94
  70.1 1.4 fusion.90
  73.3 1.8 fusion.93
  76.4 1.4 fusion.90
  79.6 1.8 fusion.93
  82.8 1.4 fusion.90
  86.0 1.8 fusion.93
  89.1 1.4 fusion.90
  92.4 1.8 fusion.93
  95.5 1.4 fusion.90
  98.7 1.8 fusion.93
  101.9 1.4 fusion.90
  105.1 1.8 fusion.93
  108.2 1.4 fusion.90
  111.4 1.8 fusion.93
  114.6 1.4 fusion.90
  117.8 1.8 fusion.93
  121.0 3.2 %copy.93 = bf16[8,640,2,128]{1,3,0,2:T(8,128)(2,1)S(1)} copy(bf16[8,640,2,128]{3,1,2,0:T(8,128)(2,1)} %get-tuple-element.48) | data formatting | bytes 5242880 | tf_op jit(solution)/shard_map/while | solution.py:94
  124.1 1.5 slice.30
  125.7 6.2 %copy.94 = bf16[1,512,2,1024]{3,2,0,1:T(2,128)(2,1)} copy(bf16[1,512,2,1024]{1,3,2,0:T(8,128)(2,1)} %bitcast.153) | data formatting | bytes 4194304 | tf_op jit(solution)/shard_map/reshape | solution.py:99
  131.9 29.2 %all_to_all.40 = bf16[1,512,2,1024]{3,2,0,1:T(2,128)(2,1)S(1)} all-to-all(bf16[1,512,2,1024]{3,2,0,1:T(2,128)(2,1)} %copy.94), channel_id=1, replica_groups=mesh['ctx'=4,'pair'=4,'dp'=2] {'ctx'}, dimensions={1} | all-to-all | bytes 4194304 | tf_op jit(solution)/shard_map/all_to_all | solution.py:100
  161.1 3.1 %reduce_sum.39 = bf16[128,2,1024]{2,1,0:T(2,128)(2,1)S(1)} reduce(bf16[4,128,2,1024]{3,2,1,0:T(2,128)(2,1)S(1)} %bitcast.152, bf16[]{:T(256)} %constant.29.clone.1), dimensions={0}, to_apply=%region_5.6 | reduce | flops 786432 | bytes 2621442 | tf_op jit(solution)/shard_map/reduce_sum | solution.py:101
  164.2 1.9 copy.95
  166.1 4.6 %all-to-all-start.2 = ((bf16[1,128,2,1024]{1,2,0,3:T(2,128)(2,1)}), bf16[1,128,2,1024]{1,2,0,3:T(2,128)(2,1)S(1)}, u32[]{:S(2)}, u32[]{:S(2)}) async-start(bf16[1,128,2,1024]{1,2,0,3:T(2,128)(2,1)} %copy.95), calls=%async_computation.2 | async-start | bytes 1048576 | tf_op jit(solution)/shard_map/all_to_all | solution.py:102
  171.3 1.2 reshape.115
  174.5 9.3 %all-to-all-done.2 = bf16[1,128,2,1024]{1,2,0,3:T(2,128)(2,1)S(1)} async-done(((bf16[1,128,2,1024]{1,2,0,3:T(2,128)(2,1)}), bf16[1,128,2,1024]{1,2,0,3:T(2,128)(2,1)S(1)}, u32[]{:S(2)}, u32[]{:S(2)}) %all-to-all-start.2) | async-done | bytes 524320 | tf_op jit(solution)/shard_map/all_to_all | solution.py:102
  184.5 1.2 copy.98
  (116 shorter events, 33.0 us)
Async XLA Ops:
  7.2 1.4 copy-start
  7.2 59.9 %all-gather.2.cloned.1.call-start = ((), (), s32[]{:S(2)}) async-start(), calls=%async_computation.3 | async-start | bytes 2621440 | tf_op jit(solution)/shard_map/all_gather | solution.py:15
  10.2 22.4 %copy-start.1 = (bf16[1,1,128,2048]{3,2,1,0:T(8,128)(2,1)S(1)}, bf16[1,1,128,2048]{3,2,1,0:T(8,128)(2,1)}, u32[]{:S(2)}) copy-start(bf16[1,1,128,2048]{3,2,1,0:T(8,128)(2,1)} %param.10) | copy-start | bytes 1572868
  10.7 22.2 %copy-start.4 = (bf16[1,1,128,1024]{3,2,1,0:T(8,128)(2,1)S(1)}, bf16[1,1,128,1024]{3,2,1,0:T(8,128)(2,1)}, u32[]{:S(2)}) copy-start(bf16[1,1,128,1024]{3,2,1,0:T(8,128)(2,1)} %param.11) | copy-start | bytes 786436
  10.8 22.4 %copy-start.5 = (bf16[1,1,128,1024]{3,2,1,0:T(8,128)(2,1)S(1)}, bf16[1,1,128,1024]{3,2,1,0:T(8,128)(2,1)}, u32[]{:S(2)}) copy-start(bf16[1,1,128,1024]{3,2,1,0:T(8,128)(2,1)} %param.12) | copy-start | bytes 786436
  31.5 1.8 copy-start.2
  32.6 1.6 copy-start.7
  161.1 9.6 %copy-start.6 = (s32[4]{0:T(128)S(1)}, s32[4]{0:T(128)}, u32[]{:S(2)}) copy-start(s32[4]{0:T(128)} %param.17) | copy-start | bytes 52
  161.1 9.7 %copy-start.3 = (bf16[8,2,128,128]{3,2,1,0:T(8,128)(2,1)S(1)}, bf16[8,2,128,128]{3,2,1,0:T(8,128)(2,1)}, u32[]{:S(2)}) copy-start(bf16[8,2,128,128]{3,2,1,0:T(8,128)(2,1)} %get-tuple-element.47) | copy-start | bytes 1572868
  166.1 17.7 %all-to-all-start.2 = ((bf16[1,128,2,1024]{1,2,0,3:T(2,128)(2,1)}), bf16[1,128,2,1024]{1,2,0,3:T(2,128)(2,1)S(1)}, u32[]{:S(2)}, u32[]{:S(2)}) async-start(bf16[1,128,2,1024]{1,2,0,3:T(2,128)(2,1)} %copy.95), calls=%async_computation.2 | async-start | bytes 1048576 | tf_op jit(solution)/shard_map/all_to_all | solution.py:102
Sparse Core Ops, SparseCore 0:
  32.7 34.2 all-gather.1
where the time goes:
time: 194 us; the launch traced here: 193 us
  blocking collectives  50 us (26%)
  waiting for transfers between devices  41.1 us (21%)
  matrix products  34.8 us (18%)
  local copies, waits for them, and re-layouts  31.2 us (16%)
  other arithmetic  15.5 us (8%)
  between operations  14.9 us (8%)
  starting transfers between devices  4.64 us (2%)
    all_gather x1, waiting for transfers between devices, gather_rows(): return lax.all_gather(kv_part, 'ctx', axis=1, tiled=True)  31.8 us
    all_to_all x1, blocking collectives, shards(): lax.all_to_all(prefix_part, 'ctx', split_axis=1, concat_axis=0, tiled=True)  29.2 us
    all_to_all x1, blocking collectives, pick_prompt(): lax.all_to_all(outgoing, 'pair', split_axis=0, concat_axis=3, tiled=True)  20.7 us
    dot_general x8, matrix products, one_head(): jnp.einsum('jqk,kd->jqd', ds_low, key_rows, preferred_element_type=jnp.fl...  14.4 us
    sub x8, matrix products, one_head(): raised = jnp.exp(scores - row_peak)  11.3 us
    all_to_all x1, waiting for transfers between devices, shards(): lax.all_to_all(ctx_total[None], 'pair', split_axis=3, concat_axis=0, tile...  9.32 us
    dynamic_slice x16, local copies, waits for them, and re-layouts, shards(): lax.map(one_head, (keys_heads, values_heads, query_heads, grad_heads))  7.76 us
    reshape x1, local copies, waits for them, and re-layouts, shards(): jnp.transpose(kv_grads[:, :pre_rows], (1, 2, 0, 3))  6.24 us
  transfers between devices with their start and end apart: 2, of which 2 were waited for; matrix products, arithmetic and copies ran while one was open for 3% of the time, Pallas kernels for 0%

commit v1 on v0

--- a/solution.py
+++ b/solution.py
@@ -12,7 +12,38 @@
 
 
 def gather_rows(kv_part):
-    return lax.all_gather(kv_part, "ctx", axis=1, tiled=True)
+
+    def push_tokens(block_in):
+        link_axis = "ctx"
+        met_up = lax.psum(1, link_axis)
+        state_now = lax.axis_index(link_axis)
+        right_arr, high, piece_out = (met_up, state_now, block_in.shape[1])
+        bank = [dev * right_arr if src_i == 1 else dev for src_i, dev in enumerate(block_in.shape)]
+        then = lax.dynamic_update_slice_in_dim(
+            jnp.zeros(bank, block_in.dtype), block_in, high * piece_out, axis=1
+        )
+        s_next = f_next = block_in
+        for m in [*range(1, right_arr // 2 + 1)]:
+            s_next = lax.ppermute(
+                s_next,
+                link_axis,
+                perm=[(src_i, (src_i + 1) % right_arr) for src_i in range(right_arr)],
+            )
+            then = lax.dynamic_update_slice_in_dim(
+                then, s_next, (high - m) % right_arr * piece_out, axis=1
+            )
+            if 2 * m < right_arr:
+                f_next = lax.ppermute(
+                    f_next,
+                    axis_name=link_axis,
+                    perm=[(src_i, (src_i - 1) % right_arr) for src_i in range(right_arr)],
+                )
+                then = lax.dynamic_update_slice_in_dim(
+                    then, f_next, (high + m) % right_arr * piece_out, axis=1
+                )
+        return then
+
+    return push_tokens(kv_part)
 
 
 def pick_prompt(kv_part, pair_prompt):

time: 194 us -> 177 us (0.912)
  blocking collectives: 50 us -> 27.5 us
  between operations: 14.9 us -> 1.55 us
  waiting for transfers between devices: 41.1 us -> 51 us
  starting transfers between devices: 4.64 us -> 13.5 us
    all_gather x1 -> x0, waiting for transfers between devices: 31.8 us -> none  [gather_rows(): return lax.all_gather(kv_part, 'ctx', axis=1, tiled=True)]
    ppermute x0 -> x3, waiting for transfers between devices: none -> 29.3 us  [the longest x2 20.2 us: push_tokens(): lax.ppermute(s_next, link_axis, perm=[(src_i, (src_i + 1) % right_arr) fo...]
    all_to_all x1 -> x0, blocking collectives: 20.7 us -> none  [pick_prompt(): lax.all_to_all(outgoing, 'pair', split_axis=0, concat_axis=3, tiled=True)]
    all_to_all x0 -> x1, waiting for transfers between devices: none -> 13.7 us  [pick_prompt(): lax.all_to_all(outgoing, 'pair', split_axis=0, concat_axis=3, tiled=True)]
    all_to_all x0 -> x1, starting transfers between devices: none -> 6.45 us  [pick_prompt(): lax.all_to_all(outgoing, 'pair', split_axis=0, concat_axis=3, tiled=True)]
    ppermute x0 -> x3, starting transfers between devices: none -> 3.57 us  [the longest x2 2.14 us: push_tokens(): lax.ppermute(s_next, link_axis, perm=[(src_i, (src_i + 1) % right_arr) fo...]
  transfers between devices with their start and end apart: 2 -> 5, of which waited for: 2 -> 5; matrix products, arithmetic and copies ran while one was open for 3% -> 4% of each run, Pallas kernels for 0% -> 0%
where the time goes in v1:
time: 177 us; the launch traced here: 176 us
  waiting for transfers between devices  51 us (29%)
  matrix products  34.8 us (20%)
  local copies, waits for them, and re-layouts  30.7 us (17%)
  blocking collectives  27.5 us (16%)
  other arithmetic  16.3 us (9%)
  starting transfers between devices  13.5 us (8%)
    all_to_all x1, blocking collectives, shards(): lax.all_to_all(prefix_part, 'ctx', split_axis=1, concat_axis=0, tiled=True)  27.5 us
    ppermute x2, waiting for transfers between devices, push_tokens(): lax.ppermute(s_next, link_axis, perm=[(src_i, (src_i + 1) % right_arr) fo...  20.2 us
    dot_general x8, matrix products, one_head(): jnp.einsum('jqk,kd->jqd', ds_low, key_rows, preferred_element_type=jnp.fl...  14.4 us
    all_to_all x1, waiting for transfers between devices, pick_prompt(): lax.all_to_all(outgoing, 'pair', split_axis=0, concat_axis=3, tiled=True)  13.7 us
    sub x8, matrix products, one_head(): raised = jnp.exp(scores - row_peak)  11.3 us
    ppermute x1, waiting for transfers between devices, push_tokens(): lax.ppermute(f_next, axis_name=link_axis, perm=[(src_i, (src_i - 1) % rig...  9.14 us
    all_to_all x1, waiting for transfers between devices, shards(): lax.all_to_all(ctx_total[None], 'pair', split_axis=3, concat_axis=0, tile...  8 us
    dynamic_slice x16, local copies, waits for them, and re-layouts, shards(): lax.map(one_head, (keys_heads, values_heads, query_heads, grad_heads))  7.75 us
  transfers between devices with their start and end apart: 5, of which 5 were waited for; matrix products, arithmetic and copies ran while one was open for 4% of the time, Pallas kernels for 0%

profile of v1, /device:TPU:0, one launch (start us, length us, event | category | flops | bytes accessed | tf_op | source)
XLA Modules:
  0.0 175.8 jit_solution(16630813539073967170)
XLA Ops:
  2.0 1.6 gather_fusion
  5.0 6.4 %all-to-all-start = ((bf16[4,128,2,256]{3,2,1,0:T(2,128)(2,1)}), bf16[4,128,2,256]{3,2,1,0:T(2,128)(2,1)S(1)}, u32[]{:S(2)}, u32[]{:S(2)}) async-start(bf16[4,128,2,256]{3,2,1,0:T(2,128)(2,1)} %broadcast_select_fusion), calls=%async_computation | async-start | bytes 1048576 | tf_op jit(solution)/shard_map/all_to_all | solution.py:51
  12.2 13.7 %all-to-all-done = bf16[4,128,2,256]{3,2,1,0:T(2,128)(2,1)S(1)} async-done(((bf16[4,128,2,256]{3,2,1,0:T(2,128)(2,1)}), bf16[4,128,2,256]{3,2,1,0:T(2,128)(2,1)S(1)}, u32[]{:S(2)}, u32[]{:S(2)}) %all-to-all-start) | async-done | bytes 524320 | tf_op jit(solution)/shard_map/all_to_all | solution.py:51
  26.4 1.5 collective-permute-start
  29.7 1.4 collective-permute-start.1
  31.2 11.1 %collective-permute-done = bf16[1,128,2,1024]{1,3,2,0:T(8,128)(2,1)} collective-permute-done((bf16[1,128,2,1024]{1,3,2,0:T(8,128)(2,1)S(1)}, bf16[1,128,2,1024]{1,3,2,0:T(8,128)(2,1)}, u32[]{:S(2)}, u32[]{:S(2)}) %collective-permute-start) | collective-permute-done | bytes 524320 | tf_op jit(solution)/shard_map/ppermute | solution.py:27
  44.4 9.1 %collective-permute-done.1 = bf16[1,128,2,1024]{1,3,2,0:T(8,128)(2,1)S(1)} collective-permute-done((bf16[1,128,2,1024]{1,3,2,0:T(8,128)(2,1)S(1)}, bf16[1,128,2,1024]{1,3,2,0:T(8,128)(2,1)S(1)}, u32[]{:S(2)}, u32[]{:S(2)}) %collective-permute-start.1) | collective-permute-done | bytes 524320 | tf_op jit(solution)/shard_map/ppermute | solution.py:36
  53.6 9.1 %collective-permute-done.2 = bf16[1,128,2,1024]{1,3,2,0:T(8,128)(2,1)S(1)} collective-permute-done((bf16[1,128,2,1024]{1,3,2,0:T(8,128)(2,1)}, bf16[1,128,2,1024]{1,3,2,0:T(8,128)(2,1)S(1)}, u32[]{:S(2)}, u32[]{:S(2)}) %collective-permute-start.2) | collective-permute-done | bytes 524320 | tf_op jit(solution)/shard_map/ppermute | solution.py:27
  64.3 50.9 %while.12 = (s32[]{:T(128)}, bf16[8,2,128,128]{3,2,1,0:T(8,128)(2,1)}, bf16[8,640,2,128]{3,1,2,0:T(8,128)(2,1)}, pred[128,640]{1,0:T(8,128)(4,1)S(1)}, bf16[8,2,...) while((s32[]{:T(128)}, ...), condition=%wide.region_4.5_spmd, body=%wide.region_0.4_spmd.sunk | while | flops 254427520 | bytes 6446201 | solution.py:125
  64.3 1.4 fusion.90
  67.5 1.8 %fusion.93 = bf16[8,2,128,128]{3,2,1,0:T(8,128)(2,1)} fusion(bf16[8,2,128,128]{3,2,1,0:T(8,128)(2,1)} %get-tuple-element.180, s32[]{:T(128)S(6)} %copy.122, bf16[2,128,640]{2,1,0:T(8,128)(2,1)S(1)} %fusion.92, bf16[8,640,128]{1,2,0:T(8,128)(2,1)} %get-tuple-element.193), kind=kOutput, calls=%fused_computation.20.clone.1 | convolution fusion | flops 42008576 | bytes 558080 | tf_op jit(solution)/shard_map/while/body/eval_jaxpr/jqk,kd->jqd/dot_general | solution.py:112
  70.7 1.4 fusion.90
  73.9 1.8 %fusion.93 = bf16[8,2,128,128]{3,2,1,0:T(8,128)(2,1)} fusion(bf16[8,2,128,128]{3,2,1,0:T(8,128)(2,1)} %get-tuple-element.180, s32[]{:T(128)S(6)} %copy.122, bf16[2,128,640]{2,1,0:T(8,128)(2,1)S(1)} %fusion.92, bf16[8,640,128]{1,2,0:T(8,128)(2,1)} %get-tuple-element.193), kind=kOutput, calls=%fused_computation.20.clone.1 | convolution fusion | flops 42008576 | bytes 558080 | tf_op jit(solution)/shard_map/while/body/eval_jaxpr/jqk,kd->jqd/dot_general | solution.py:112
  77.0 1.4 fusion.90
  80.2 1.8 %fusion.93 = bf16[8,2,128,128]{3,2,1,0:T(8,128)(2,1)} fusion(bf16[8,2,128,128]{3,2,1,0:T(8,128)(2,1)} %get-tuple-element.180, s32[]{:T(128)S(6)} %copy.122, bf16[2,128,640]{2,1,0:T(8,128)(2,1)S(1)} %fusion.92, bf16[8,640,128]{1,2,0:T(8,128)(2,1)} %get-tuple-element.193), kind=kOutput, calls=%fused_computation.20.clone.1 | convolution fusion | flops 42008576 | bytes 558080 | tf_op jit(solution)/shard_map/while/body/eval_jaxpr/jqk,kd->jqd/dot_general | solution.py:112
  86.6 1.8 %fusion.93 = bf16[8,2,128,128]{3,2,1,0:T(8,128)(2,1)} fusion(bf16[8,2,128,128]{3,2,1,0:T(8,128)(2,1)} %get-tuple-element.180, s32[]{:T(128)S(6)} %copy.122, bf16[2,128,640]{2,1,0:T(8,128)(2,1)S(1)} %fusion.92, bf16[8,640,128]{1,2,0:T(8,128)(2,1)} %get-tuple-element.193), kind=kOutput, calls=%fused_computation.20.clone.1 | convolution fusion | flops 42008576 | bytes 558080 | tf_op jit(solution)/shard_map/while/body/eval_jaxpr/jqk,kd->jqd/dot_general | solution.py:112
  89.7 1.4 fusion.90
  92.9 1.8 %fusion.93 = bf16[8,2,128,128]{3,2,1,0:T(8,128)(2,1)} fusion(bf16[8,2,128,128]{3,2,1,0:T(8,128)(2,1)} %get-tuple-element.180, s32[]{:T(128)S(6)} %copy.122, bf16[2,128,640]{2,1,0:T(8,128)(2,1)S(1)} %fusion.92, bf16[8,640,128]{1,2,0:T(8,128)(2,1)} %get-tuple-element.193), kind=kOutput, calls=%fused_computation.20.clone.1 | convolution fusion | flops 42008576 | bytes 558080 | tf_op jit(solution)/shard_map/while/body/eval_jaxpr/jqk,kd->jqd/dot_general | solution.py:112
  96.1 1.4 fusion.90
  99.3 1.8 %fusion.93 = bf16[8,2,128,128]{3,2,1,0:T(8,128)(2,1)} fusion(bf16[8,2,128,128]{3,2,1,0:T(8,128)(2,1)} %get-tuple-element.180, s32[]{:T(128)S(6)} %copy.122, bf16[2,128,640]{2,1,0:T(8,128)(2,1)S(1)} %fusion.92, bf16[8,640,128]{1,2,0:T(8,128)(2,1)} %get-tuple-element.193), kind=kOutput, calls=%fused_computation.20.clone.1 | convolution fusion | flops 42008576 | bytes 558080 | tf_op jit(solution)/shard_map/while/body/eval_jaxpr/jqk,kd->jqd/dot_general | solution.py:112
  102.4 1.4 fusion.90
  105.6 1.8 %fusion.93 = bf16[8,2,128,128]{3,2,1,0:T(8,128)(2,1)} fusion(bf16[8,2,128,128]{3,2,1,0:T(8,128)(2,1)} %get-tuple-element.180, s32[]{:T(128)S(6)} %copy.122, bf16[2,128,640]{2,1,0:T(8,128)(2,1)S(1)} %fusion.92, bf16[8,640,128]{1,2,0:T(8,128)(2,1)} %get-tuple-element.193), kind=kOutput, calls=%fused_computation.20.clone.1 | convolution fusion | flops 42008576 | bytes 558080 | tf_op jit(solution)/shard_map/while/body/eval_jaxpr/jqk,kd->jqd/dot_general | solution.py:112
  108.8 1.4 fusion.90
  112.0 1.8 %fusion.93 = bf16[8,2,128,128]{3,2,1,0:T(8,128)(2,1)} fusion(bf16[8,2,128,128]{3,2,1,0:T(8,128)(2,1)} %get-tuple-element.180, s32[]{:T(128)S(6)} %copy.122, bf16[2,128,640]{2,1,0:T(8,128)(2,1)S(1)} %fusion.92, bf16[8,640,128]{1,2,0:T(8,128)(2,1)} %get-tuple-element.193), kind=kOutput, calls=%fused_computation.20.clone.1 | convolution fusion | flops 42008576 | bytes 558080 | tf_op jit(solution)/shard_map/while/body/eval_jaxpr/jqk,kd->jqd/dot_general | solution.py:112
  115.2 3.2 %copy.97 = bf16[8,640,2,128]{1,3,0,2:T(8,128)(2,1)S(1)} copy(bf16[8,640,2,128]{3,1,2,0:T(8,128)(2,1)} %get-tuple-element.48) | data formatting | bytes 5242880 | tf_op jit(solution)/shard_map/while | solution.py:125
  118.4 1.5 slice.30
  119.9 6.3 %copy.98 = bf16[1,512,2,1024]{3,2,0,1:T(2,128)(2,1)} copy(bf16[1,512,2,1024]{1,3,2,0:T(8,128)(2,1)} %bitcast.159) | data formatting | bytes 4194304 | tf_op jit(solution)/shard_map/reshape | solution.py:130
  126.2 27.5 %all_to_all.39 = bf16[1,512,2,1024]{3,2,0,1:T(2,128)(2,1)S(1)} all-to-all(bf16[1,512,2,1024]{3,2,0,1:T(2,128)(2,1)} %copy.98), channel_id=1, replica_groups=mesh['ctx'=4,'pair'=4,'dp'=2] {'ctx'}, dimensions={1} | all-to-all | bytes 4194304 | tf_op jit(solution)/shard_map/all_to_all | solution.py:131
  153.7 3.1 %reduce_sum.39 = bf16[128,2,1024]{2,1,0:T(2,128)(2,1)S(1)} reduce(bf16[4,128,2,1024]{3,2,1,0:T(2,128)(2,1)S(1)} %bitcast.158, bf16[]{:T(256)} %constant.78.clone.1), dimensions={0}, to_apply=%region_5.6 | reduce | flops 786432 | bytes 2621442 | tf_op jit(solution)/shard_map/reduce_sum | solution.py:132
  156.8 1.9 %copy.99 = bf16[1,128,2,1024]{1,2,0,3:T(2,128)(2,1)} copy(bf16[1,128,2,1024]{3,2,1,0:T(2,128)(2,1)S(1)} %bitcast.168) | data formatting | bytes 1048576 | tf_op jit(solution)/shard_map/broadcast_in_dim | solution.py:133
  158.7 3.5 %all-to-all-start.2 = ((bf16[1,128,2,1024]{1,2,0,3:T(2,128)(2,1)}), bf16[1,128,2,1024]{1,2,0,3:T(2,128)(2,1)S(1)}, u32[]{:S(2)}, u32[]{:S(2)}) async-start(bf16[1,128,2,1024]{1,2,0,3:T(2,128)(2,1)} %copy.99), calls=%async_computation.2 | async-start | bytes 1048576 | tf_op jit(solution)/shard_map/all_to_all | solution.py:133
  165.9 8.0 %all-to-all-done.2 = bf16[1,128,2,1024]{1,2,0,3:T(2,128)(2,1)S(1)} async-done(((bf16[1,128,2,1024]{1,2,0,3:T(2,128)(2,1)}), bf16[1,128,2,1024]{1,2,0,3:T(2,128)(2,1)S(1)}, u32[]{:S(2)}, u32[]{:S(2)}) %all-to-all-start.2) | async-done | bytes 524320 | tf_op jit(solution)/shard_map/all_to_all | solution.py:133
  (125 shorter events, 40.6 us)
Async XLA Ops:
  0.6 1.4 copy-start
  0.6 11.5 %copy-start.7 = (s32[1,1,4]{2,1,0:T(1,128)S(1)}, s32[1,1,4]{2,1,0:T(1,128)}, u32[]{:S(2)}) copy-start(s32[1,1,4]{2,1,0:T(1,128)} %param.15) | copy-start | bytes 52
  2.0 25.9 %copy-start.1 = (bf16[1,1,128,2048]{3,2,1,0:T(8,128)(2,1)S(1)}, bf16[1,1,128,2048]{3,2,1,0:T(8,128)(2,1)}, u32[]{:S(2)}) copy-start(bf16[1,1,128,2048]{3,2,1,0:T(8,128)(2,1)} %param.10) | copy-start | bytes 1572868
  3.7 24.6 %copy-start.4 = (bf16[1,1,128,1024]{3,2,1,0:T(8,128)(2,1)S(1)}, bf16[1,1,128,1024]{3,2,1,0:T(8,128)(2,1)}, u32[]{:S(2)}) copy-start(bf16[1,1,128,1024]{3,2,1,0:T(8,128)(2,1)} %param.11) | copy-start | bytes 786436
  5.0 23.4 %copy-start.5 = (bf16[1,1,128,1024]{3,2,1,0:T(8,128)(2,1)S(1)}, bf16[1,1,128,1024]{3,2,1,0:T(8,128)(2,1)}, u32[]{:S(2)}) copy-start(bf16[1,1,128,1024]{3,2,1,0:T(8,128)(2,1)} %param.12) | copy-start | bytes 786436
  5.0 23.6 %copy-start.2 = (bf16[1,1,128,2048]{3,2,1,0:T(8,128)(2,1)S(1)}, bf16[1,1,128,2048]{3,2,1,0:T(8,128)(2,1)}, u32[]{:S(2)}) copy-start(bf16[1,1,128,2048]{3,2,1,0:T(8,128)(2,1)} %param.13) | copy-start | bytes 1572868
  5.0 20.9 %all-to-all-start = ((bf16[4,128,2,256]{3,2,1,0:T(2,128)(2,1)}), bf16[4,128,2,256]{3,2,1,0:T(2,128)(2,1)S(1)}, u32[]{:S(2)}, u32[]{:S(2)}) async-start(bf16[4,128,2,256]{3,2,1,0:T(2,128)(2,1)} %broadcast_select_fusion), calls=%async_computation | async-start | bytes 1048576 | tf_op jit(solution)/shard_map/all_to_all | solution.py:51
  26.4 15.9 %collective-permute-start = (bf16[1,128,2,1024]{1,3,2,0:T(8,128)(2,1)S(1)}, bf16[1,128,2,1024]{1,3,2,0:T(8,128)(2,1)}, u32[]{:S(2)}, u32[]{:S(2)}) collective-permute-start(bf16[1,128,2,1024]{1,3,2,0:T(8,128)(2,1)S(1)} %bitcast.163), channel_id=1, source_target_pairs={{0,8},{8,16},{16,24},{24,0},{1,9},{9,17},{17,25},{25,1},{2,10},{10... | collective-permute-start | bytes 1572872 | tf_op jit(solution)/shard_map/ppermute | solution.py:27
  29.7 23.8 %collective-permute-start.1 = (bf16[1,128,2,1024]{1,3,2,0:T(8,128)(2,1)S(1)}, bf16[1,128,2,1024]{1,3,2,0:T(8,128)(2,1)S(1)}, u32[]{:S(2)}, u32[]{:S(2)}) collective-permute-start(bf16[1,128,2,1024]{1,3,2,0:T(8,128)(2,1)S(1)} %bitcast.164), channel_id=1, source_target_pairs={{0,24},{8,0},{16,8},{24,16},{1,25},{9,1},{17,9},{25,17},{2,26},{10... | collective-permute-start | bytes 1572872 | tf_op jit(solution)/shard_map/ppermute | solution.py:36
  42.3 20.4 %collective-permute-start.2 = (bf16[1,128,2,1024]{1,3,2,0:T(8,128)(2,1)}, bf16[1,128,2,1024]{1,3,2,0:T(8,128)(2,1)S(1)}, u32[]{:S(2)}, u32[]{:S(2)}) collective-permute-start(bf16[1,128,2,1024]{1,3,2,0:T(8,128)(2,1)} %collective-permute-done), channel_id=1, source_target_pairs={{0,8},{8,16},{16,24},{24,0},{1,9},{9,17},{17,25},{25,1},{2,10},{10... | collective-permute-start | bytes 1572872 | tf_op jit(solution)/shard_map/ppermute | solution.py:27
  153.7 8.5 %copy-start.6 = (s32[4]{0:T(128)S(1)}, s32[4]{0:T(128)}, u32[]{:S(2)}) copy-start(s32[4]{0:T(128)} %param.17) | copy-start | bytes 52
  153.7 8.5 %copy-start.3 = (bf16[8,2,128,128]{3,2,1,0:T(8,128)(2,1)S(1)}, bf16[8,2,128,128]{3,2,1,0:T(8,128)(2,1)}, u32[]{:S(2)}) copy-start(bf16[8,2,128,128]{3,2,1,0:T(8,128)(2,1)} %get-tuple-element.47) | copy-start | bytes 1572868
  158.7 15.2 %all-to-all-start.2 = ((bf16[1,128,2,1024]{1,2,0,3:T(2,128)(2,1)}), bf16[1,128,2,1024]{1,2,0,3:T(2,128)(2,1)S(1)}, u32[]{:S(2)}, u32[]{:S(2)}) async-start(bf16[1,128,2,1024]{1,2,0,3:T(2,128)(2,1)} %copy.99), calls=%async_computation.2 | async-start | bytes 1048576 | tf_op jit(solution)/shard_map/all_to_all | solution.py:133
